TPU v7x, 128 devices: a whole 4x4x4 slice. The times are simulated.
128 devices in a mesh: head: 4 (over z), page: 32 (over x, y, core).
Axes of the slice: x: 4, y: 4, z: 4, core: 2. Of those that a mesh axis runs over, the one named last changes fastest.
Arguments:
- hidden_in: bfloat16 [32, 1024, 1024], P('page', 'head'), may hold values from -6 to 6
- norm_gain: float32 [1024], replicated, may hold values from 0.1 to 1.9
- w_qkv: bfloat16 [1024, 3, 1024], P(None, None, 'head'), may hold values from -0.1875 to 0.1875
- w_out: bfloat16 [1024, 1024], P('head'), may hold values from -0.75 to 0.75
- cache_kv: bfloat16 [2, 64, 128, 1024], P(None, 'page', None, 'head'), may hold values from -110 to 110, as said below
- page_node: int32 [64], replicated, may hold values from 0 to 18, as said below
- page_fill: int32 [64], replicated, may hold values from 1 to 128
- node_parent: int32 [19], replicated, may hold values from 0 to 2, as said below
- tok_seg: int32 [32, 1024], P('page'), may hold values from 0 to 7, never falling along the last dimension, each value on 1 to 256 neighbouring positions
- req_leaf: int32 [32, 8], P('page'), may hold values from 3 to 18, as said below
Outputs:
- attn_out: bfloat16 [32, 1024, 1024], P('page', 'head')
Inputs may be any that keep to these rules, and one draw needn't show every extreme that they name: `cache_kv`: entries of the cache; keys and values. `page_node`: every node owns at least one page. `node_parent`: node 0 is the root and its own parent; nodes 1 to 2 have parent 0; the others have a parent among nodes 1 to 2, and each of those has a child. `req_leaf`: each request names a lowest-level node; every lowest-level node is named by some request.
All inputs are finite; a program needn't handle non-finite values.
Results may differ from a plain program's by a relative error of at most 0.018.
Values may be sent and summed in bfloat16 or wider, within the bound.
No kernel may reach another device: no remote copies, remote signals or barrier semaphores. Data moves between devices by JAX's collectives and lax.ppermute only.
A program may use at most 64 MiB of HBM per device.

v0:
```python
import math
import jax
import jax.numpy as jnp
from jax import lax
from jax.sharding import PartitionSpec as P

HD = 64
EPSILON = 1e-06
FLOOR_SCORE = -1e30


def lookup(indices, lookup_table):
    matches = indices[:, None] == jnp.arange(lookup_table.shape[0], dtype=jnp.int32)[None, :]
    return jnp.sum(jnp.where(matches, lookup_table[None, :], 0), axis=1)


def shards(
    hidden_in,
    norm_gain,
    w_qkv,
    w_out,
    cache_kv,
    page_node,
    page_fill,
    node_parent,
    tok_seg,
    req_leaf,
):
    widened = hidden_in[0].astype(jnp.float32)
    normed = (
        widened
        * lax.rsqrt(jnp.mean(widened * widened, axis=1, keepdims=True) + EPSILON)
        * norm_gain
    ).astype(jnp.bfloat16)
    model_width = widened.shape[1]
    group_width = w_qkv.shape[2]
    head_size = HD
    group_heads = group_width // head_size
    weight_flat = w_qkv.reshape(model_width, 3 * group_width)
    projected = jnp.dot(
        lax.all_gather(normed, "head", axis=0, tiled=True),
        weight_flat,
        preferred_element_type=jnp.float32,
    ).astype(jnp.bfloat16)
    queries_all = projected.shape[0]
    queries = projected[:, :group_width].reshape(queries_all, group_heads, head_size)
    key_new = projected[:, group_width : 2 * group_width].reshape(
        queries_all, group_heads, head_size
    )
    value_new = projected[:, 2 * group_width :].reshape(queries_all, group_heads, head_size)
    score_scale = head_size ** (-0.5)
    segment = tok_seg[0]
    leaf_node = lookup(segment, req_leaf[0])
    upper_node = lookup(leaf_node, node_parent)
    root_node = lookup(upper_node, node_parent)
    position = jnp.arange(queries_all, dtype=jnp.int32)
    block_rows = min(queries_all, 512)

    def suffix_block(first):
        query_rows = lax.dynamic_slice_in_dim(queries, first, block_rows, 0)
        segment_rows = lax.dynamic_slice_in_dim(segment, first, block_rows, 0)
        position_rows = first + jnp.arange(block_rows, dtype=jnp.int32)
        visible = (segment_rows[:, None] == segment[None, :]) & (
            position[None, :] <= position_rows[:, None]
        )
        scores = (
            jnp.einsum("qhd,khd->hqk", query_rows, key_new, preferred_element_type=jnp.float32)
            * score_scale
        )
        scores = jnp.where(visible[None], scores, FLOOR_SCORE)
        row_max = jnp.max(scores, axis=2)
        weights = jnp.where(visible[None], jnp.exp(scores - row_max[:, :, None]), 0.0)
        row_sum = jnp.sum(weights, axis=2)
        weighted = jnp.einsum(
            "hqk,khd->hqd",
            weights.astype(jnp.bfloat16),
            value_new,
            preferred_element_type=jnp.float32,
        )
        return (row_max, row_sum, weighted)

    block_starts = jnp.arange(0, queries_all, block_rows, dtype=jnp.int32)
    block_max, block_sum, block_weighted = lax.map(suffix_block, block_starts)
    initial = (
        jnp.transpose(block_max, (1, 0, 2)).reshape(group_heads, queries_all),
        jnp.transpose(block_sum, (1, 0, 2)).reshape(group_heads, queries_all),
        jnp.transpose(block_weighted, (1, 0, 2, 3)).reshape(group_heads, queries_all, head_size),
    )
    page_len = cache_kv.shape[2]
    page_slot = jnp.arange(page_len, dtype=jnp.int32)
    shard_piece = lax.all_gather(cache_kv, "page", axis=1, tiled=True)
    piece_pages = shard_piece.shape[1]
    group_pages = math.gcd(piece_pages, 4)
    step_count = piece_pages // group_pages
    block_keys = group_pages * page_len
    key_blocks = shard_piece[0].reshape(step_count, block_keys, group_heads, head_size)
    value_blocks = shard_piece[1].reshape(step_count, block_keys, group_heads, head_size)
    key_nodes = jnp.repeat(page_node, page_len).reshape(step_count, block_keys)
    key_valid = (page_slot[None, :] < page_fill[:, None]).reshape(step_count, block_keys)

    def one_step(partial_value, inputs):
        row_max, row_sum, weighted = partial_value
        key_block, value_block, node_block, valid_block = inputs
        visible = (
            (node_block[None, :] == leaf_node[:, None])
            | (node_block[None, :] == upper_node[:, None])
            | (node_block[None, :] == root_node[:, None])
        ) & valid_block[None, :]
        scores = (
            jnp.einsum("qhd,khd->hqk", queries, key_block, preferred_element_type=jnp.float32)
            * score_scale
        )
        scores = jnp.where(visible[None], scores, FLOOR_SCORE)
        new_max = jnp.maximum(row_max, jnp.max(scores, axis=2))
        rescale = jnp.exp(row_max - new_max)
        weights = jnp.where(visible[None], jnp.exp(scores - new_max[:, :, None]), 0.0)
        row_sum = row_sum * rescale + jnp.sum(weights, axis=2)
        weighted = weighted * rescale[:, :, None] + jnp.einsum(
            "hqk,khd->hqd",
            weights.astype(jnp.bfloat16),
            value_block,
            preferred_element_type=jnp.float32,
        )
        return ((new_max, row_sum, weighted), None)

    result_state, unused = lax.scan(
        one_step, initial, (key_blocks, value_blocks, key_nodes, key_valid)
    )
    final_max, final_sum, final_weighted = result_state
    attention = (final_weighted / final_sum[:, :, None]).astype(jnp.bfloat16)
    attention = jnp.transpose(attention, (1, 0, 2)).reshape(queries_all, group_width)
    result = lax.psum_scatter(
        jnp.dot(attention, w_out, preferred_element_type=jnp.float32).astype(jnp.bfloat16),
        "head",
        scatter_dimension=0,
        tiled=True,
    )
    return result[None]


def solution(mesh):
    placed = (
        P("page", "head", None),
        P(),
        P(None, None, "head"),
        P("head", None),
        P(None, "page", None, "head"),
        P(),
        P(),
        P(),
        P("page", None),
        P("page", None),
    )
    return jax.shard_map(
        shards, mesh=mesh, in_specs=placed, out_specs=P("page", "head", None), check_vma=False
    )
```

profile of v0, /device:TPU:1, one launch (start us, length us, event | category | flops | bytes accessed | tf_op | source)
XLA Modules:
  0.0 339.6 jit_solution(15440758614901769843)
XLA Ops:
  16.4 27.6 %all-gather.3.cloned.1.call-done = bf16[1024,1024]{1,0:T(8,128)(2,1)} async-done(((bf16[256,1024]{1,0:T(8,128)(2,1)}), bf16[1024,1024]{1,0:T(8,128)(2,1)}) %all-gather.3.cloned.1.call-update) | async-done | bytes 2097168 | tf_op jit(solution)/shard_map/all_gather | solution.py:41
  44.1 3.4 %convolution_convert_fusion.1 = bf16[1024,768]{0,1:T(8,128)(2,1)S(1)} fusion(bf16[1024,1024]{1,0:T(8,128)(2,1)} %all-gather.3.cloned.1.call-done, bf16[1024,768]{0,1:T(8,128)(2,1)S(1)} %bitcast.106), kind=kOutput, calls=%fused_computation.45 | convolution fusion | flops 1611399168 | bytes 5242880 | tf_op jit(solution)/shard_map/dot_general | solution.py:40
  48.4 24.0 %while.30 = (s32[]{:T(128)}, f32[2,4,512]{2,1,0:T(4,128)S(1)}, f32[2,4,512]{2,1,0:T(4,128)S(1)}, f32[2,4,512,64]{2,3,1,0:T(8,128)S(1)}, s32[2]{0:T(128)S(1)}, /*...) while((s32[]{:T(128)}, f32[2,4,512]{2,1,0:T(4,128)S(1)}, ...), condition=%wide.region_4.5_spmd.clone, body=%wide.region_1.4_spmd.clone.sunk | while | flops 565703168 | bytes 29178048 | solution.py:83
  53.9 3.5 %fusion.77 = f32[2,4,512,64]{2,3,1,0:T(8,128)S(1)} fusion(f32[2,4,512,64]{2,3,1,0:T(8,128)S(1)} %get-tuple-element.401, s32[]{:T(128)} %get-tuple-element.398, bf16[1024,4,64]{0,2,1:T(8,128)(2,1)} %get-tuple-element.420, f32[4,512,1024]{2,1,0:T(8,128)S(1)} %get-tuple-element.381, f32[4,512]{1,0:T(4,128)S(1)} %get-tuple-element.382, ...), kind=kOutput, calls=%fused_computation.11.clone.1 | convolution fusion | flops 278921216 | bytes 9969668 | tf_op jit(solution)/shard_map/while/body/eval_jaxpr/hqk,khd->hqd/dot_general | solution.py:74
  57.4 2.9 fusion.76
  65.9 3.5 %fusion.77 = f32[2,4,512,64]{2,3,1,0:T(8,128)S(1)} fusion(f32[2,4,512,64]{2,3,1,0:T(8,128)S(1)} %get-tuple-element.401, s32[]{:T(128)} %get-tuple-element.398, bf16[1024,4,64]{0,2,1:T(8,128)(2,1)} %get-tuple-element.420, f32[4,512,1024]{2,1,0:T(8,128)S(1)} %get-tuple-element.381, f32[4,512]{1,0:T(4,128)S(1)} %get-tuple-element.382, ...), kind=kOutput, calls=%fused_computation.11.clone.1 | convolution fusion | flops 278921216 | bytes 9969668 | tf_op jit(solution)/shard_map/while/body/eval_jaxpr/hqk,khd->hqd/dot_general | solution.py:74
  69.4 2.9 fusion.76
  72.5 27.1 %all-gather.5.cloned.1.call-done = bf16[2,64,128,256]{3,2,1,0:T(8,128)(2,1)} async-done(((bf16[2,2,128,256]{3,2,1,0:T(8,128)(2,1)}), bf16[2,64,128,256]{3,2,1,0:T(8,128)(2,1)}) %all-gather.5.cloned.1.call-update) | async-done | bytes 8388624 | tf_op jit(solution)/shard_map/all_gather | solution.py:91
  99.5 6.0 %fusion.43 = (bf16[1,64,128,256]{3,2,1,0:T(8,128)(2,1)}, bf16[1,64,128,256]{3,2,1,0:T(8,128)(2,1)}) fusion(bf16[2,64,128,256]{3,2,1,0:T(8,128)(2,1)} %all-gather.5.cloned.1.call-done), kind=kLoop, calls=%fused_computation.63 | loop fusion | bytes 16777216 | tf_op jit(solution)/shard_map/slice | solution.py:97
  105.5 12.9 %reshape.224 = bf16[16,512,4,64]{3,2,1,0:T(4,128)(2,1)} reshape(bf16[1,64,128,256]{3,2,1,0:T(8,128)(2,1)} %get-tuple-element.231) | data formatting | bytes 8388608 | tf_op jit(solution)/shard_map/reshape;squeeze | solution.py:96
  118.4 12.7 %copy.24 = bf16[16,512,4,64]{1,3,2,0:T(8,128)(2,1)} copy(bf16[16,512,4,64]{3,2,1,0:T(4,128)(2,1)} %reshape.224) | data formatting | bytes 8388608 | tf_op jit(solution)/shard_map/while | solution.py:126
  131.1 12.9 %reshape.225 = bf16[16,512,4,64]{3,2,1,0:T(4,128)(2,1)} reshape(bf16[1,64,128,256]{3,2,1,0:T(8,128)(2,1)} %get-tuple-element.230) | data formatting | bytes 8388608 | tf_op jit(solution)/shard_map/reshape;squeeze | solution.py:97
  144.0 12.7 %copy.25 = bf16[16,512,4,64]{1,3,2,0:T(8,128)(2,1)} copy(bf16[16,512,4,64]{3,2,1,0:T(4,128)(2,1)} %reshape.225) | data formatting | bytes 8388608 | tf_op jit(solution)/shard_map/while | solution.py:126
  156.7 145.0 %while.29 = (s32[]{:T(128)}, f32[4,1024]{1,0:T(4,128)S(1)}, f32[4,1024]{1,0:T(4,128)S(1)}, f32[4,1024,64]{1,2,0:T(8,128)S(1)}, s32[16,512]{1,0:T(8,128)S(1)}, /*...) while((s32[]{:T(128)}, f32[4,1024]{1,0:T(4,128)S(1)}, ...), condition=%wide.region_11.12_spmd, body=%wide.region_8.11_spmd.sunk | while | flops 567812096 | bytes 30691972 | solution.py:126
  157.3 2.6 fusion.68
  159.9 2.1 fusion.69
  162.0 3.6 %fusion.70 = f32[4,1024,64]{1,2,0:T(8,128)S(1)} fusion(f32[4,512,1024]{2,1,0:T(8,128)S(1)} %get-tuple-element.368, f32[4,1024]{1,0:T(4,128)S(1)} %max.4, pred[1024,512]{0,1:T(8,128)(4,1)S(1)} %or_and_fusion.2, f32[4,1024,64]{1,2,0:T(8,128)S(1)} %get-tuple-element.440, f32[4,1024]{1,0:T(4,128)S(1)} %get-tuple-element.370, ...), kind=kOutput, calls=%fused_computation.29.clone.1 | convolution fusion | flops 279445504 | bytes 11305472 | tf_op jit(solution)/shard_map/while/body/eval_jaxpr/hqk,khd->hqd/dot_general | solution.py:118
  166.4 2.6 fusion.68
  171.1 3.6 %fusion.70 = f32[4,1024,64]{1,2,0:T(8,128)S(1)} fusion(f32[4,512,1024]{2,1,0:T(8,128)S(1)} %get-tuple-element.368, f32[4,1024]{1,0:T(4,128)S(1)} %max.4, pred[1024,512]{0,1:T(8,128)(4,1)S(1)} %or_and_fusion.2, f32[4,1024,64]{1,2,0:T(8,128)S(1)} %get-tuple-element.440, f32[4,1024]{1,0:T(4,128)S(1)} %get-tuple-element.370, ...), kind=kOutput, calls=%fused_computation.29.clone.1 | convolution fusion | flops 279445504 | bytes 11305472 | tf_op jit(solution)/shard_map/while/body/eval_jaxpr/hqk,khd->hqd/dot_general | solution.py:118
  175.5 2.6 fusion.68
  180.2 3.6 %fusion.70 = f32[4,1024,64]{1,2,0:T(8,128)S(1)} fusion(f32[4,512,1024]{2,1,0:T(8,128)S(1)} %get-tuple-element.368, f32[4,1024]{1,0:T(4,128)S(1)} %max.4, pred[1024,512]{0,1:T(8,128)(4,1)S(1)} %or_and_fusion.2, f32[4,1024,64]{1,2,0:T(8,128)S(1)} %get-tuple-element.440, f32[4,1024]{1,0:T(4,128)S(1)} %get-tuple-element.370, ...), kind=kOutput, calls=%fused_computation.29.clone.1 | convolution fusion | flops 279445504 | bytes 11305472 | tf_op jit(solution)/shard_map/while/body/eval_jaxpr/hqk,khd->hqd/dot_general | solution.py:118
  184.5 2.6 fusion.68
  189.2 3.6 %fusion.70 = f32[4,1024,64]{1,2,0:T(8,128)S(1)} fusion(f32[4,512,1024]{2,1,0:T(8,128)S(1)} %get-tuple-element.368, f32[4,1024]{1,0:T(4,128)S(1)} %max.4, pred[1024,512]{0,1:T(8,128)(4,1)S(1)} %or_and_fusion.2, f32[4,1024,64]{1,2,0:T(8,128)S(1)} %get-tuple-element.440, f32[4,1024]{1,0:T(4,128)S(1)} %get-tuple-element.370, ...), kind=kOutput, calls=%fused_computation.29.clone.1 | convolution fusion | flops 279445504 | bytes 11305472 | tf_op jit(solution)/shard_map/while/body/eval_jaxpr/hqk,khd->hqd/dot_general | solution.py:118
  193.6 2.6 fusion.68
  198.3 3.6 %fusion.70 = f32[4,1024,64]{1,2,0:T(8,128)S(1)} fusion(f32[4,512,1024]{2,1,0:T(8,128)S(1)} %get-tuple-element.368, f32[4,1024]{1,0:T(4,128)S(1)} %max.4, pred[1024,512]{0,1:T(8,128)(4,1)S(1)} %or_and_fusion.2, f32[4,1024,64]{1,2,0:T(8,128)S(1)} %get-tuple-element.440, f32[4,1024]{1,0:T(4,128)S(1)} %get-tuple-element.370, ...), kind=kOutput, calls=%fused_computation.29.clone.1 | convolution fusion | flops 279445504 | bytes 11305472 | tf_op jit(solution)/shard_map/while/body/eval_jaxpr/hqk,khd->hqd/dot_general | solution.py:118
  202.6 2.6 fusion.68
  207.4 3.6 %fusion.70 = f32[4,1024,64]{1,2,0:T(8,128)S(1)} fusion(f32[4,512,1024]{2,1,0:T(8,128)S(1)} %get-tuple-element.368, f32[4,1024]{1,0:T(4,128)S(1)} %max.4, pred[1024,512]{0,1:T(8,128)(4,1)S(1)} %or_and_fusion.2, f32[4,1024,64]{1,2,0:T(8,128)S(1)} %get-tuple-element.440, f32[4,1024]{1,0:T(4,128)S(1)} %get-tuple-element.370, ...), kind=kOutput, calls=%fused_computation.29.clone.1 | convolution fusion | flops 279445504 | bytes 11305472 | tf_op jit(solution)/shard_map/while/body/eval_jaxpr/hqk,khd->hqd/dot_general | solution.py:118
  211.7 2.6 fusion.68
  216.4 3.6 %fusion.70 = f32[4,1024,64]{1,2,0:T(8,128)S(1)} fusion(f32[4,512,1024]{2,1,0:T(8,128)S(1)} %get-tuple-element.368, f32[4,1024]{1,0:T(4,128)S(1)} %max.4, pred[1024,512]{0,1:T(8,128)(4,1)S(1)} %or_and_fusion.2, f32[4,1024,64]{1,2,0:T(8,128)S(1)} %get-tuple-element.440, f32[4,1024]{1,0:T(4,128)S(1)} %get-tuple-element.370, ...), kind=kOutput, calls=%fused_computation.29.clone.1 | convolution fusion | flops 279445504 | bytes 11305472 | tf_op jit(solution)/shard_map/while/body/eval_jaxpr/hqk,khd->hqd/dot_general | solution.py:118
  220.8 2.6 fusion.68
  225.5 3.6 %fusion.70 = f32[4,1024,64]{1,2,0:T(8,128)S(1)} fusion(f32[4,512,1024]{2,1,0:T(8,128)S(1)} %get-tuple-element.368, f32[4,1024]{1,0:T(4,128)S(1)} %max.4, pred[1024,512]{0,1:T(8,128)(4,1)S(1)} %or_and_fusion.2, f32[4,1024,64]{1,2,0:T(8,128)S(1)} %get-tuple-element.440, f32[4,1024]{1,0:T(4,128)S(1)} %get-tuple-element.370, ...), kind=kOutput, calls=%fused_computation.29.clone.1 | convolution fusion | flops 279445504 | bytes 11305472 | tf_op jit(solution)/shard_map/while/body/eval_jaxpr/hqk,khd->hqd/dot_general | solution.py:118
  229.8 2.6 fusion.68
  234.5 3.6 %fusion.70 = f32[4,1024,64]{1,2,0:T(8,128)S(1)} fusion(f32[4,512,1024]{2,1,0:T(8,128)S(1)} %get-tuple-element.368, f32[4,1024]{1,0:T(4,128)S(1)} %max.4, pred[1024,512]{0,1:T(8,128)(4,1)S(1)} %or_and_fusion.2, f32[4,1024,64]{1,2,0:T(8,128)S(1)} %get-tuple-element.440, f32[4,1024]{1,0:T(4,128)S(1)} %get-tuple-element.370, ...), kind=kOutput, calls=%fused_computation.29.clone.1 | convolution fusion | flops 279445504 | bytes 11305472 | tf_op jit(solution)/shard_map/while/body/eval_jaxpr/hqk,khd->hqd/dot_general | solution.py:118
  238.9 2.6 fusion.68
  243.6 3.6 %fusion.70 = f32[4,1024,64]{1,2,0:T(8,128)S(1)} fusion(f32[4,512,1024]{2,1,0:T(8,128)S(1)} %get-tuple-element.368, f32[4,1024]{1,0:T(4,128)S(1)} %max.4, pred[1024,512]{0,1:T(8,128)(4,1)S(1)} %or_and_fusion.2, f32[4,1024,64]{1,2,0:T(8,128)S(1)} %get-tuple-element.440, f32[4,1024]{1,0:T(4,128)S(1)} %get-tuple-element.370, ...), kind=kOutput, calls=%fused_computation.29.clone.1 | convolution fusion | flops 279445504 | bytes 11305472 | tf_op jit(solution)/shard_map/while/body/eval_jaxpr/hqk,khd->hqd/dot_general | solution.py:118
  247.9 2.6 fusion.68
  252.7 3.6 %fusion.70 = f32[4,1024,64]{1,2,0:T(8,128)S(1)} fusion(f32[4,512,1024]{2,1,0:T(8,128)S(1)} %get-tuple-element.368, f32[4,1024]{1,0:T(4,128)S(1)} %max.4, pred[1024,512]{0,1:T(8,128)(4,1)S(1)} %or_and_fusion.2, f32[4,1024,64]{1,2,0:T(8,128)S(1)} %get-tuple-element.440, f32[4,1024]{1,0:T(4,128)S(1)} %get-tuple-element.370, ...), kind=kOutput, calls=%fused_computation.29.clone.1 | convolution fusion | flops 279445504 | bytes 11305472 | tf_op jit(solution)/shard_map/while/body/eval_jaxpr/hqk,khd->hqd/dot_general | solution.py:118
  257.0 2.6 fusion.68
  261.7 3.6 %fusion.70 = f32[4,1024,64]{1,2,0:T(8,128)S(1)} fusion(f32[4,512,1024]{2,1,0:T(8,128)S(1)} %get-tuple-element.368, f32[4,1024]{1,0:T(4,128)S(1)} %max.4, pred[1024,512]{0,1:T(8,128)(4,1)S(1)} %or_and_fusion.2, f32[4,1024,64]{1,2,0:T(8,128)S(1)} %get-tuple-element.440, f32[4,1024]{1,0:T(4,128)S(1)} %get-tuple-element.370, ...), kind=kOutput, calls=%fused_computation.29.clone.1 | convolution fusion | flops 279445504 | bytes 11305472 | tf_op jit(solution)/shard_map/while/body/eval_jaxpr/hqk,khd->hqd/dot_general | solution.py:118
  266.1 2.6 fusion.68
  270.8 3.6 %fusion.70 = f32[4,1024,64]{1,2,0:T(8,128)S(1)} fusion(f32[4,512,1024]{2,1,0:T(8,128)S(1)} %get-tuple-element.368, f32[4,1024]{1,0:T(4,128)S(1)} %max.4, pred[1024,512]{0,1:T(8,128)(4,1)S(1)} %or_and_fusion.2, f32[4,1024,64]{1,2,0:T(8,128)S(1)} %get-tuple-element.440, f32[4,1024]{1,0:T(4,128)S(1)} %get-tuple-element.370, ...), kind=kOutput, calls=%fused_computation.29.clone.1 | convolution fusion | flops 279445504 | bytes 11305472 | tf_op jit(solution)/shard_map/while/body/eval_jaxpr/hqk,khd->hqd/dot_general | solution.py:118
  275.1 2.6 fusion.68
  279.8 3.6 %fusion.70 = f32[4,1024,64]{1,2,0:T(8,128)S(1)} fusion(f32[4,512,1024]{2,1,0:T(8,128)S(1)} %get-tuple-element.368, f32[4,1024]{1,0:T(4,128)S(1)} %max.4, pred[1024,512]{0,1:T(8,128)(4,1)S(1)} %or_and_fusion.2, f32[4,1024,64]{1,2,0:T(8,128)S(1)} %get-tuple-element.440, f32[4,1024]{1,0:T(4,128)S(1)} %get-tuple-element.370, ...), kind=kOutput, calls=%fused_computation.29.clone.1 | convolution fusion | flops 279445504 | bytes 11305472 | tf_op jit(solution)/shard_map/while/body/eval_jaxpr/hqk,khd->hqd/dot_general | solution.py:118
  284.2 2.6 fusion.68
  288.9 3.6 %fusion.70 = f32[4,1024,64]{1,2,0:T(8,128)S(1)} fusion(f32[4,512,1024]{2,1,0:T(8,128)S(1)} %get-tuple-element.368, f32[4,1024]{1,0:T(4,128)S(1)} %max.4, pred[1024,512]{0,1:T(8,128)(4,1)S(1)} %or_and_fusion.2, f32[4,1024,64]{1,2,0:T(8,128)S(1)} %get-tuple-element.440, f32[4,1024]{1,0:T(4,128)S(1)} %get-tuple-element.370, ...), kind=kOutput, calls=%fused_computation.29.clone.1 | convolution fusion | flops 279445504 | bytes 11305472 | tf_op jit(solution)/shard_map/while/body/eval_jaxpr/hqk,khd->hqd/dot_general | solution.py:118
  293.3 2.6 fusion.68
  298.0 3.6 %fusion.70 = f32[4,1024,64]{1,2,0:T(8,128)S(1)} fusion(f32[4,512,1024]{2,1,0:T(8,128)S(1)} %get-tuple-element.368, f32[4,1024]{1,0:T(4,128)S(1)} %max.4, pred[1024,512]{0,1:T(8,128)(4,1)S(1)} %or_and_fusion.2, f32[4,1024,64]{1,2,0:T(8,128)S(1)} %get-tuple-element.440, f32[4,1024]{1,0:T(4,128)S(1)} %get-tuple-element.370, ...), kind=kOutput, calls=%fused_computation.29.clone.1 | convolution fusion | flops 279445504 | bytes 11305472 | tf_op jit(solution)/shard_map/while/body/eval_jaxpr/hqk,khd->hqd/dot_general | solution.py:118
  303.9 29.2 %reduce-scatter.2.cloned.1.call-done = bf16[256,1024]{1,0:T(8,128)(2,1)} async-done(((bf16[1024,1024]{1,0:T(8,128)(2,1)}), bf16[256,1024]{1,0:T(8,128)(2,1)}) %reduce-scatter.2.cloned.1.call-update) | async-done | bytes 524304 | tf_op jit(solution)/shard_map/reduce_scatter | solution.py:132
  (155 shorter events, 63.2 us)
Async XLA Ops:
  6.5 295.2 %copy-start = (bf16[256,1024]{1,0:T(8,128)(2,1)S(1)}, bf16[256,1024]{1,0:T(8,128)(2,1)}, u32[]{:S(2)}) copy-start(bf16[256,1024]{1,0:T(8,128)(2,1)} %param.17) | copy-start | bytes 1572868
  6.5 37.5 %all-gather.3.cloned.1.call-start = ((), (), s32[]{:S(2)}) async-start(), calls=%async_computation.1 | async-start | bytes 2621440 | tf_op jit(solution)/shard_map/all_gather | solution.py:41
  9.9 89.7 %all-gather.5.cloned.1.call-start = ((), (), s32[]{:S(2)}) async-start(), calls=%async_computation.2 | async-start | bytes 8650752 | tf_op jit(solution)/shard_map/all_gather | solution.py:91
  10.6 322.5 %reduce-scatter.2.cloned.1.call-start = ((), (), s32[]{:S(2)}) async-start(), calls=%async_computation.3 | async-start | bytes 2621440 | tf_op jit(solution)/shard_map/reduce_scatter | solution.py:132
  10.7 37.7 %copy-start.1 = (s32[1,1024]{1,0:T(1,128)S(1)}, s32[1,1024]{1,0:T(1,128)}, u32[]{:S(2)}) copy-start(s32[1,1024]{1,0:T(1,128)} %param.22) | copy-start | bytes 12292
Sparse Core Ops, SparseCore 0:
  10.0 34.0 all-gather.2
  46.4 53.0 all-gather.4
  304.0 29.0 reduce-scatter.1
where the time goes:
time: 342 us; the launch traced here: 340 us
  matrix products  116 us (34%)
  waiting for transfers between devices  84.7 us (25%)
  local copies, waits for them, and re-layouts  63.5 us (19%)
  other arithmetic  57.9 us (17%)
  between operations  13.2 us (4%)
  loops' own time  4.56 us (1%)
    dot_general x16, matrix products, one_step(): jnp.einsum('hqk,khd->hqd', weights.astype(jnp.bfloat16), value_block, pre...  58.4 us
    dot_general x16, matrix products, one_step(): jnp.einsum('qhd,khd->hqk', queries, key_block, preferred_element_type=jnp...  40.8 us
    reduce_sum x16, other arithmetic, one_step(): row_sum = row_sum * rescale + jnp.sum(weights, axis=2)  33.7 us
    reduce_scatter x1, waiting for transfers between devices, shards(): lax.psum_scatter(jnp.dot(attention, w_out, preferred_element_type=jnp.flo...  29.2 us
    all_gather x1, waiting for transfers between devices, shards(): lax.all_gather(normed, 'head', axis=0, tiled=True)  27.6 us
    all_gather x1, waiting for transfers between devices, shards(): shard_piece = lax.all_gather(cache_kv, 'page', axis=1, tiled=True)  27.1 us
    while x2, local copies, waits for them, and re-layouts, shards(): lax.scan(one_step, initial, (key_blocks, value_blocks, key_nodes, key_val...  25.4 us
    another operation x1, local copies, waits for them, and re-layouts, shards(): shard_piece[0].reshape(step_count, block_keys, group_heads, head_size)  12.9 us
  transfers between devices with their start and end apart: 3, of which 3 were waited for; matrix products, arithmetic and copies ran while one was open for 9% of the time, Pallas kernels for 0%

commit v1 on v0

--- a/solution.py
+++ b/solution.py
@@ -37,10 +37,17 @@
     head_size = HD
     group_heads = group_width // head_size
     weight_flat = w_qkv.reshape(model_width, 3 * group_width)
+    close_shifts_all = lambda my_data, named_axis, axis_k: jnp.concatenate(
+        lax.all_to_all(
+            jnp.stack(lax.axis_size(named_axis) * [my_data]),
+            concat_axis=0,
+            axis_name=named_axis,
+            split_axis=0,
+        ),
+        axis=axis_k,
+    )
     projected = jnp.dot(
-        lax.all_gather(normed, "head", axis=0, tiled=True),
-        weight_flat,
-        preferred_element_type=jnp.float32,
+        close_shifts_all(normed, "head", 0), weight_flat, preferred_element_type=jnp.float32
     ).astype(jnp.bfloat16)
     queries_all = projected.shape[0]
     queries = projected[:, :group_width].reshape(queries_all, group_heads, head_size)

time: 342 us -> 317 us (0.927)
  waiting for transfers between devices: 84.7 us -> 53.6 us
  starting transfers between devices: 0.08 us -> 5.88 us
    all_gather x1 -> x0, waiting for transfers between devices: 27.6 us -> none  [shards(): lax.all_gather(normed, 'head', axis=0, tiled=True)]
    all_gather x1, waiting for transfers between devices: 27.1 us -> 0.02 us  [shards(): shard_piece = lax.all_gather(cache_kv, 'page', axis=1, tiled=True)]
    all_to_all x0 -> x1, waiting for transfers between devices: none -> 22.2 us  [shards(): lax.all_to_all(jnp.stack(lax.axis_size(named_axis) * [my_data]), concat_a...]
    all_to_all x0 -> x1, starting transfers between devices: none -> 5.84 us  [shards(): lax.all_to_all(jnp.stack(lax.axis_size(named_axis) * [my_data]), concat_a...]
  transfers between devices with their start and end apart: 3 -> 3, of which waited for: 3 -> 2; matrix products, arithmetic and copies ran while one was open for 9% -> 11% of each run, Pallas kernels for 0% -> 0%
where the time goes in v1:
time: 317 us; the launch traced here: 314 us
  matrix products  116 us (37%)
  local copies, waits for them, and re-layouts  66 us (21%)
  other arithmetic  55 us (17%)
  waiting for transfers between devices  53.6 us (17%)
  between operations  13.6 us (4%)
  starting transfers between devices  5.88 us (2%)
  loops' own time  4.61 us (1%)
    dot_general x16, matrix products, one_step(): jnp.einsum('hqk,khd->hqd', weights.astype(jnp.bfloat16), value_block, pre...  58.4 us
    dot_general x16, matrix products, one_step(): jnp.einsum('qhd,khd->hqk', queries, key_block, preferred_element_type=jnp...  40.8 us
    reduce_sum x16, other arithmetic, one_step(): row_sum = row_sum * rescale + jnp.sum(weights, axis=2)  33.7 us
    reduce_scatter x1, waiting for transfers between devices, shards(): lax.psum_scatter(jnp.dot(attention, w_out, preferred_element_type=jnp.flo...  30.7 us
    while x2, local copies, waits for them, and re-layouts, shards(): lax.scan(one_step, initial, (key_blocks, value_blocks, key_nodes, key_val...  25.4 us
    all_to_all x1, waiting for transfers between devices, shards(): lax.all_to_all(jnp.stack(lax.axis_size(named_axis) * [my_data]), concat_a...  22.2 us
    another operation x1, local copies, waits for them, and re-layouts, shards(): shard_piece[0].reshape(step_count, block_keys, group_heads, head_size)  12.9 us
    another operation x1, local copies, waits for them, and re-layouts, shards(): shard_piece[1].reshape(step_count, block_keys, group_heads, head_size)  12.9 us
  transfers between devices with their start and end apart: 3, of which 2 were waited for; matrix products, arithmetic and copies ran while one was open for 11% of the time, Pallas kernels for 0%

profile of v1, /device:TPU:1, one launch (start us, length us, event | category | flops | bytes accessed | tf_op | source)
XLA Modules:
  0.0 314.2 jit_solution(2536403732086591634)
XLA Ops:
  11.4 5.8 %all-to-all-start = ((bf16[4,256,1024]{2,1,0:T(8,128)(2,1)}), bf16[4,256,1024]{2,1,0:T(8,128)(2,1)S(1)}, u32[]{:S(2)}, u32[]{:S(2)}) async-start(bf16[4,256,1024]{2,1,0:T(8,128)(2,1)} %stack.10), calls=%async_computation | async-start | bytes 4194304 | tf_op jit(solution)/shard_map/all_to_all | solution.py:41
  17.3 2.6 copy.20
  20.6 22.2 %all-to-all-done = bf16[4,256,1024]{2,1,0:T(8,128)(2,1)S(1)} async-done(((bf16[4,256,1024]{2,1,0:T(8,128)(2,1)}), bf16[4,256,1024]{2,1,0:T(8,128)(2,1)S(1)}, u32[]{:S(2)}, u32[]{:S(2)}) %all-to-all-start) | async-done | bytes 2097184 | tf_op jit(solution)/shard_map/all_to_all | solution.py:41
  42.8 3.2 %convolution_convert_fusion.1 = bf16[1024,768]{0,1:T(8,128)(2,1)S(1)} fusion(bf16[1024,1024]{1,0:T(8,128)(2,1)S(1)} %bitcast.103, bf16[1024,768]{0,1:T(8,128)(2,1)} %bitcast.106), kind=kOutput, calls=%fused_computation.45 | convolution fusion | flops 1611399168 | bytes 5242880 | tf_op jit(solution)/shard_map/dot_general | solution.py:49
  46.9 24.1 %while.30 = (s32[]{:T(128)}, f32[2,4,512]{2,1,0:T(4,128)S(1)}, f32[2,4,512]{2,1,0:T(4,128)S(1)}, f32[2,4,512,64]{2,3,1,0:T(8,128)}, s32[2]{0:T(128)S(1)}, /*inde...) while((s32[]{:T(128)}, f32[2,4,512]{2,1,0:T(4,128)S(1)}, ...), condition=%wide.region_4.5_spmd.clone, body=%wide.region_1.4_spmd.clone.sunk | while | flops 565703168 | bytes 37566712 | solution.py:90
  52.4 3.5 %fusion.78 = f32[2,4,512,64]{2,3,1,0:T(8,128)S(1)} fusion(f32[2,4,512,64]{2,3,1,0:T(8,128)S(1)} %copy-done.1, s32[]{:T(128)} %get-tuple-element.398, bf16[1024,4,64]{0,2,1:T(8,128)(2,1)} %get-tuple-element.420, f32[4,512,1024]{2,1,0:T(8,128)S(1)} %get-tuple-element.381, f32[4,512]{1,0:T(4,128)S(1)} %get-tuple-element.382, ...), kind=kOutput, calls=%fused_computation.11.clone.1 | convolution fusion | flops 278921216 | bytes 9969668 | tf_op jit(solution)/shard_map/while/body/eval_jaxpr/hqk,khd->hqd/dot_general | solution.py:81
  56.0 2.9 fusion.77
  64.5 3.6 %fusion.78 = f32[2,4,512,64]{2,3,1,0:T(8,128)S(1)} fusion(f32[2,4,512,64]{2,3,1,0:T(8,128)S(1)} %copy-done.1, s32[]{:T(128)} %get-tuple-element.398, bf16[1024,4,64]{0,2,1:T(8,128)(2,1)} %get-tuple-element.420, f32[4,512,1024]{2,1,0:T(8,128)S(1)} %get-tuple-element.381, f32[4,512]{1,0:T(4,128)S(1)} %get-tuple-element.382, ...), kind=kOutput, calls=%fused_computation.11.clone.1 | convolution fusion | flops 278921216 | bytes 9969668 | tf_op jit(solution)/shard_map/while/body/eval_jaxpr/hqk,khd->hqd/dot_general | solution.py:81
  68.0 2.9 fusion.77
  72.3 6.0 %fusion.44 = (bf16[1,64,128,256]{3,2,1,0:T(8,128)(2,1)}, bf16[1,64,128,256]{3,2,1,0:T(8,128)(2,1)}) fusion(bf16[2,64,128,256]{3,2,1,0:T(8,128)(2,1)} %all-gather.2.cloned.1.call-done), kind=kLoop, calls=%fused_computation.64 | loop fusion | bytes 16777216 | tf_op jit(solution)/shard_map/slice | solution.py:104
  78.3 12.9 %reshape.241 = bf16[16,512,4,64]{3,2,1,0:T(4,128)(2,1)} reshape(bf16[1,64,128,256]{3,2,1,0:T(8,128)(2,1)} %get-tuple-element.231) | data formatting | bytes 8388608 | tf_op jit(solution)/shard_map/reshape;squeeze | solution.py:103
  91.2 12.7 %copy.24 = bf16[16,512,4,64]{1,3,2,0:T(8,128)(2,1)} copy(bf16[16,512,4,64]{3,2,1,0:T(4,128)(2,1)} %reshape.241) | data formatting | bytes 8388608 | tf_op jit(solution)/shard_map/while | solution.py:133
  103.9 12.9 %reshape.242 = bf16[16,512,4,64]{3,2,1,0:T(4,128)(2,1)} reshape(bf16[1,64,128,256]{3,2,1,0:T(8,128)(2,1)} %get-tuple-element.230) | data formatting | bytes 8388608 | tf_op jit(solution)/shard_map/reshape;squeeze | solution.py:104
  116.8 12.7 %copy.25 = bf16[16,512,4,64]{1,3,2,0:T(8,128)(2,1)} copy(bf16[16,512,4,64]{3,2,1,0:T(4,128)(2,1)} %reshape.242) | data formatting | bytes 8388608 | tf_op jit(solution)/shard_map/while | solution.py:133
  129.5 145.0 %while.29 = (s32[]{:T(128)}, f32[4,1024]{1,0:T(4,128)S(1)}, f32[4,1024]{1,0:T(4,128)S(1)}, f32[4,1024,64]{1,2,0:T(8,128)S(1)}, s32[16,512]{1,0:T(8,128)S(1)}, /*...) while((s32[]{:T(128)}, f32[4,1024]{1,0:T(4,128)S(1)}, ...), condition=%wide.region_11.12_spmd, body=%wide.region_8.11_spmd.sunk | while | flops 567812096 | bytes 30691972 | solution.py:133
  130.1 2.6 fusion.69
  134.8 3.6 %fusion.71 = f32[4,1024,64]{1,2,0:T(8,128)S(1)} fusion(f32[4,512,1024]{2,1,0:T(8,128)S(1)} %get-tuple-element.368, f32[4,1024]{1,0:T(4,128)S(1)} %max.4, pred[1024,512]{0,1:T(8,128)(4,1)S(1)} %or_and_fusion.2, f32[4,1024,64]{1,2,0:T(8,128)S(1)} %get-tuple-element.440, f32[4,1024]{1,0:T(4,128)S(1)} %get-tuple-element.370, ...), kind=kOutput, calls=%fused_computation.29.clone.1 | convolution fusion | flops 279445504 | bytes 11305472 | tf_op jit(solution)/shard_map/while/body/eval_jaxpr/hqk,khd->hqd/dot_general | solution.py:125
  139.2 2.6 fusion.69
  143.9 3.6 %fusion.71 = f32[4,1024,64]{1,2,0:T(8,128)S(1)} fusion(f32[4,512,1024]{2,1,0:T(8,128)S(1)} %get-tuple-element.368, f32[4,1024]{1,0:T(4,128)S(1)} %max.4, pred[1024,512]{0,1:T(8,128)(4,1)S(1)} %or_and_fusion.2, f32[4,1024,64]{1,2,0:T(8,128)S(1)} %get-tuple-element.440, f32[4,1024]{1,0:T(4,128)S(1)} %get-tuple-element.370, ...), kind=kOutput, calls=%fused_computation.29.clone.1 | convolution fusion | flops 279445504 | bytes 11305472 | tf_op jit(solution)/shard_map/while/body/eval_jaxpr/hqk,khd->hqd/dot_general | solution.py:125
  148.3 2.6 fusion.69
  153.0 3.6 %fusion.71 = f32[4,1024,64]{1,2,0:T(8,128)S(1)} fusion(f32[4,512,1024]{2,1,0:T(8,128)S(1)} %get-tuple-element.368, f32[4,1024]{1,0:T(4,128)S(1)} %max.4, pred[1024,512]{0,1:T(8,128)(4,1)S(1)} %or_and_fusion.2, f32[4,1024,64]{1,2,0:T(8,128)S(1)} %get-tuple-element.440, f32[4,1024]{1,0:T(4,128)S(1)} %get-tuple-element.370, ...), kind=kOutput, calls=%fused_computation.29.clone.1 | convolution fusion | flops 279445504 | bytes 11305472 | tf_op jit(solution)/shard_map/while/body/eval_jaxpr/hqk,khd->hqd/dot_general | solution.py:125
  157.3 2.6 fusion.69
  162.0 3.6 %fusion.71 = f32[4,1024,64]{1,2,0:T(8,128)S(1)} fusion(f32[4,512,1024]{2,1,0:T(8,128)S(1)} %get-tuple-element.368, f32[4,1024]{1,0:T(4,128)S(1)} %max.4, pred[1024,512]{0,1:T(8,128)(4,1)S(1)} %or_and_fusion.2, f32[4,1024,64]{1,2,0:T(8,128)S(1)} %get-tuple-element.440, f32[4,1024]{1,0:T(4,128)S(1)} %get-tuple-element.370, ...), kind=kOutput, calls=%fused_computation.29.clone.1 | convolution fusion | flops 279445504 | bytes 11305472 | tf_op jit(solution)/shard_map/while/body/eval_jaxpr/hqk,khd->hqd/dot_general | solution.py:125
  166.4 2.6 fusion.69
  171.1 3.6 %fusion.71 = f32[4,1024,64]{1,2,0:T(8,128)S(1)} fusion(f32[4,512,1024]{2,1,0:T(8,128)S(1)} %get-tuple-element.368, f32[4,1024]{1,0:T(4,128)S(1)} %max.4, pred[1024,512]{0,1:T(8,128)(4,1)S(1)} %or_and_fusion.2, f32[4,1024,64]{1,2,0:T(8,128)S(1)} %get-tuple-element.440, f32[4,1024]{1,0:T(4,128)S(1)} %get-tuple-element.370, ...), kind=kOutput, calls=%fused_computation.29.clone.1 | convolution fusion | flops 279445504 | bytes 11305472 | tf_op jit(solution)/shard_map/while/body/eval_jaxpr/hqk,khd->hqd/dot_general | solution.py:125
  175.4 2.6 fusion.69
  180.2 3.6 %fusion.71 = f32[4,1024,64]{1,2,0:T(8,128)S(1)} fusion(f32[4,512,1024]{2,1,0:T(8,128)S(1)} %get-tuple-element.368, f32[4,1024]{1,0:T(4,128)S(1)} %max.4, pred[1024,512]{0,1:T(8,128)(4,1)S(1)} %or_and_fusion.2, f32[4,1024,64]{1,2,0:T(8,128)S(1)} %get-tuple-element.440, f32[4,1024]{1,0:T(4,128)S(1)} %get-tuple-element.370, ...), kind=kOutput, calls=%fused_computation.29.clone.1 | convolution fusion | flops 279445504 | bytes 11305472 | tf_op jit(solution)/shard_map/while/body/eval_jaxpr/hqk,khd->hqd/dot_general | solution.py:125
  184.5 2.6 fusion.69
  189.2 3.6 %fusion.71 = f32[4,1024,64]{1,2,0:T(8,128)S(1)} fusion(f32[4,512,1024]{2,1,0:T(8,128)S(1)} %get-tuple-element.368, f32[4,1024]{1,0:T(4,128)S(1)} %max.4, pred[1024,512]{0,1:T(8,128)(4,1)S(1)} %or_and_fusion.2, f32[4,1024,64]{1,2,0:T(8,128)S(1)} %get-tuple-element.440, f32[4,1024]{1,0:T(4,128)S(1)} %get-tuple-element.370, ...), kind=kOutput, calls=%fused_computation.29.clone.1 | convolution fusion | flops 279445504 | bytes 11305472 | tf_op jit(solution)/shard_map/while/body/eval_jaxpr/hqk,khd->hqd/dot_general | solution.py:125
  193.6 2.6 fusion.69
  198.3 3.6 %fusion.71 = f32[4,1024,64]{1,2,0:T(8,128)S(1)} fusion(f32[4,512,1024]{2,1,0:T(8,128)S(1)} %get-tuple-element.368, f32[4,1024]{1,0:T(4,128)S(1)} %max.4, pred[1024,512]{0,1:T(8,128)(4,1)S(1)} %or_and_fusion.2, f32[4,1024,64]{1,2,0:T(8,128)S(1)} %get-tuple-element.440, f32[4,1024]{1,0:T(4,128)S(1)} %get-tuple-element.370, ...), kind=kOutput, calls=%fused_computation.29.clone.1 | convolution fusion | flops 279445504 | bytes 11305472 | tf_op jit(solution)/shard_map/while/body/eval_jaxpr/hqk,khd->hqd/dot_general | solution.py:125
  202.6 2.6 fusion.69
  207.3 3.6 %fusion.71 = f32[4,1024,64]{1,2,0:T(8,128)S(1)} fusion(f32[4,512,1024]{2,1,0:T(8,128)S(1)} %get-tuple-element.368, f32[4,1024]{1,0:T(4,128)S(1)} %max.4, pred[1024,512]{0,1:T(8,128)(4,1)S(1)} %or_and_fusion.2, f32[4,1024,64]{1,2,0:T(8,128)S(1)} %get-tuple-element.440, f32[4,1024]{1,0:T(4,128)S(1)} %get-tuple-element.370, ...), kind=kOutput, calls=%fused_computation.29.clone.1 | convolution fusion | flops 279445504 | bytes 11305472 | tf_op jit(solution)/shard_map/while/body/eval_jaxpr/hqk,khd->hqd/dot_general | solution.py:125
  211.7 2.6 fusion.69
  216.4 3.6 %fusion.71 = f32[4,1024,64]{1,2,0:T(8,128)S(1)} fusion(f32[4,512,1024]{2,1,0:T(8,128)S(1)} %get-tuple-element.368, f32[4,1024]{1,0:T(4,128)S(1)} %max.4, pred[1024,512]{0,1:T(8,128)(4,1)S(1)} %or_and_fusion.2, f32[4,1024,64]{1,2,0:T(8,128)S(1)} %get-tuple-element.440, f32[4,1024]{1,0:T(4,128)S(1)} %get-tuple-element.370, ...), kind=kOutput, calls=%fused_computation.29.clone.1 | convolution fusion | flops 279445504 | bytes 11305472 | tf_op jit(solution)/shard_map/while/body/eval_jaxpr/hqk,khd->hqd/dot_general | solution.py:125
  220.7 2.6 fusion.69
  225.5 3.6 %fusion.71 = f32[4,1024,64]{1,2,0:T(8,128)S(1)} fusion(f32[4,512,1024]{2,1,0:T(8,128)S(1)} %get-tuple-element.368, f32[4,1024]{1,0:T(4,128)S(1)} %max.4, pred[1024,512]{0,1:T(8,128)(4,1)S(1)} %or_and_fusion.2, f32[4,1024,64]{1,2,0:T(8,128)S(1)} %get-tuple-element.440, f32[4,1024]{1,0:T(4,128)S(1)} %get-tuple-element.370, ...), kind=kOutput, calls=%fused_computation.29.clone.1 | convolution fusion | flops 279445504 | bytes 11305472 | tf_op jit(solution)/shard_map/while/body/eval_jaxpr/hqk,khd->hqd/dot_general | solution.py:125
  229.8 2.6 fusion.69
  234.5 3.6 %fusion.71 = f32[4,1024,64]{1,2,0:T(8,128)S(1)} fusion(f32[4,512,1024]{2,1,0:T(8,128)S(1)} %get-tuple-element.368, f32[4,1024]{1,0:T(4,128)S(1)} %max.4, pred[1024,512]{0,1:T(8,128)(4,1)S(1)} %or_and_fusion.2, f32[4,1024,64]{1,2,0:T(8,128)S(1)} %get-tuple-element.440, f32[4,1024]{1,0:T(4,128)S(1)} %get-tuple-element.370, ...), kind=kOutput, calls=%fused_computation.29.clone.1 | convolution fusion | flops 279445504 | bytes 11305472 | tf_op jit(solution)/shard_map/while/body/eval_jaxpr/hqk,khd->hqd/dot_general | solution.py:125
  238.9 2.6 fusion.69
  243.6 3.6 %fusion.71 = f32[4,1024,64]{1,2,0:T(8,128)S(1)} fusion(f32[4,512,1024]{2,1,0:T(8,128)S(1)} %get-tuple-element.368, f32[4,1024]{1,0:T(4,128)S(1)} %max.4, pred[1024,512]{0,1:T(8,128)(4,1)S(1)} %or_and_fusion.2, f32[4,1024,64]{1,2,0:T(8,128)S(1)} %get-tuple-element.440, f32[4,1024]{1,0:T(4,128)S(1)} %get-tuple-element.370, ...), kind=kOutput, calls=%fused_computation.29.clone.1 | convolution fusion | flops 279445504 | bytes 11305472 | tf_op jit(solution)/shard_map/while/body/eval_jaxpr/hqk,khd->hqd/dot_general | solution.py:125
  247.9 2.6 fusion.69
  252.6 3.6 %fusion.71 = f32[4,1024,64]{1,2,0:T(8,128)S(1)} fusion(f32[4,512,1024]{2,1,0:T(8,128)S(1)} %get-tuple-element.368, f32[4,1024]{1,0:T(4,128)S(1)} %max.4, pred[1024,512]{0,1:T(8,128)(4,1)S(1)} %or_and_fusion.2, f32[4,1024,64]{1,2,0:T(8,128)S(1)} %get-tuple-element.440, f32[4,1024]{1,0:T(4,128)S(1)} %get-tuple-element.370, ...), kind=kOutput, calls=%fused_computation.29.clone.1 | convolution fusion | flops 279445504 | bytes 11305472 | tf_op jit(solution)/shard_map/while/body/eval_jaxpr/hqk,khd->hqd/dot_general | solution.py:125
  257.0 2.6 fusion.69
  261.7 3.6 %fusion.71 = f32[4,1024,64]{1,2,0:T(8,128)S(1)} fusion(f32[4,512,1024]{2,1,0:T(8,128)S(1)} %get-tuple-element.368, f32[4,1024]{1,0:T(4,128)S(1)} %max.4, pred[1024,512]{0,1:T(8,128)(4,1)S(1)} %or_and_fusion.2, f32[4,1024,64]{1,2,0:T(8,128)S(1)} %get-tuple-element.440, f32[4,1024]{1,0:T(4,128)S(1)} %get-tuple-element.370, ...), kind=kOutput, calls=%fused_computation.29.clone.1 | convolution fusion | flops 279445504 | bytes 11305472 | tf_op jit(solution)/shard_map/while/body/eval_jaxpr/hqk,khd->hqd/dot_general | solution.py:125
  266.1 2.6 fusion.69
  270.8 3.6 %fusion.71 = f32[4,1024,64]{1,2,0:T(8,128)S(1)} fusion(f32[4,512,1024]{2,1,0:T(8,128)S(1)} %get-tuple-element.368, f32[4,1024]{1,0:T(4,128)S(1)} %max.4, pred[1024,512]{0,1:T(8,128)(4,1)S(1)} %or_and_fusion.2, f32[4,1024,64]{1,2,0:T(8,128)S(1)} %get-tuple-element.440, f32[4,1024]{1,0:T(4,128)S(1)} %get-tuple-element.370, ...), kind=kOutput, calls=%fused_computation.29.clone.1 | convolution fusion | flops 279445504 | bytes 11305472 | tf_op jit(solution)/shard_map/while/body/eval_jaxpr/hqk,khd->hqd/dot_general | solution.py:125
  276.7 30.7 %reduce-scatter.2.cloned.1.call-done = bf16[256,1024]{1,0:T(8,128)(2,1)} async-done(((bf16[1024,1024]{1,0:T(8,128)(2,1)}), bf16[256,1024]{1,0:T(8,128)(2,1)}) %reduce-scatter.2.cloned.1.call-update) | async-done | bytes 524304 | tf_op jit(solution)/shard_map/reduce_scatter | solution.py:139
  (171 shorter events, 62.3 us)
Async XLA Ops:
  6.5 268.0 %copy-start = (bf16[256,1024]{1,0:T(8,128)(2,1)S(1)}, bf16[256,1024]{1,0:T(8,128)(2,1)}, u32[]{:S(2)}) copy-start(bf16[256,1024]{1,0:T(8,128)(2,1)} %param.17) | copy-start | bytes 1572868
  6.5 13.3 %copy-start.5 = (s32[64]{0:T(128)S(1)}, s32[64]{0:T(128)}, u32[]{:S(2)}) copy-start(s32[64]{0:T(128)} %param.19) | copy-start | bytes 772
  6.5 13.5 %copy-start.6 = (s32[64]{0:T(128)S(1)}, s32[64]{0:T(128)}, u32[]{:S(2)}) copy-start(s32[64]{0:T(128)} %param.20) | copy-start | bytes 772
  6.5 13.6 %copy-start.3 = (s32[1,1024]{1,0:T(1,128)S(1)}, s32[1,1024]{1,0:T(1,128)}, u32[]{:S(2)}) copy-start(s32[1,1024]{1,0:T(1,128)} %param.22) | copy-start | bytes 12292
  6.5 13.6 %copy-start.7 = (s32[1,8]{1,0:T(1,128)S(1)}, s32[1,8]{1,0:T(1,128)}, u32[]{:S(2)}) copy-start(s32[1,8]{1,0:T(1,128)} %param.23) | copy-start | bytes 100
  6.5 13.7 %copy-start.4 = (s32[19]{0:T(128)S(1)}, s32[19]{0:T(128)}, u32[]{:S(2)}) copy-start(s32[19]{0:T(128)} %param.21) | copy-start | bytes 232
  6.6 65.8 %all-gather.2.cloned.1.call-start = ((), (), s32[]{:S(2)}) async-start(), calls=%async_computation.2 | async-start | bytes 8650752 | tf_op jit(solution)/shard_map/all_gather | solution.py:98
  11.4 31.3 %all-to-all-start = ((bf16[4,256,1024]{2,1,0:T(8,128)(2,1)}), bf16[4,256,1024]{2,1,0:T(8,128)(2,1)S(1)}, u32[]{:S(2)}, u32[]{:S(2)}) async-start(bf16[4,256,1024]{2,1,0:T(8,128)(2,1)} %stack.10), calls=%async_computation | async-start | bytes 4194304 | tf_op jit(solution)/shard_map/all_to_all | solution.py:41
  17.3 290.1 %reduce-scatter.2.cloned.1.call-start = ((), (), s32[]{:S(2)}) async-start(), calls=%async_computation.3 | async-start | bytes 2621440 | tf_op jit(solution)/shard_map/reduce_scatter | solution.py:139
  46.9 5.5 %copy-start.1 = (f32[2,4,512,64]{2,3,1,0:T(8,128)S(1)}, f32[2,4,512,64]{2,3,1,0:T(8,128)}, u32[]{:S(2)}) copy-start(f32[2,4,512,64]{2,3,1,0:T(8,128)} %get-tuple-element.401) | copy-start | bytes 3145732 | tf_op jit(solution)/shard_map/while
  56.0 2.9 copy-start.2
  58.9 5.5 %copy-start.1 = (f32[2,4,512,64]{2,3,1,0:T(8,128)S(1)}, f32[2,4,512,64]{2,3,1,0:T(8,128)}, u32[]{:S(2)}) copy-start(f32[2,4,512,64]{2,3,1,0:T(8,128)} %get-tuple-element.401) | copy-start | bytes 3145732 | tf_op jit(solution)/shard_map/while
  68.0 2.9 copy-start.2
Sparse Core Ops, SparseCore 0:
  9.7 56.2 all-gather.1
  276.8 30.5 reduce-scatter.1
